TPU v7x, 32 devices: a whole 2x2x4 slice. The times are simulated.
32 devices in a mesh: ctx: 8 (over y, x, core), tp: 4 (over z).
Axes of the slice: x: 2, y: 2, z: 4, core: 2. Of those that a mesh axis runs over, the one named last changes fastest.
Arguments:
- stream: bfloat16 [1024, 4096], P('ctx', 'tp'), may hold values from -52 to 52
- shutter: bfloat16 [1024, 4096], P('ctx', 'tp'), may hold values from -6 to 6
- feeder: bfloat16 [1024, 4096], P('ctx', 'tp'), may hold values from -6 to 6
- stencil: float32 [7, 4096], P(None, 'tp'), may hold values from -2 to 2
- valves: bfloat16 [1024, 4096], P('ctx', 'tp'), may hold values from -6 to 6
- intake: bfloat16 [1024, 4096], P('ctx', 'tp'), may hold values from -6 to 6
- kernel: float32 [128, 4096], P(None, 'tp'), may hold values from -0.5 to 0.5
- scaling: float32 [4096], P('tp'), may hold values from 0.1 to 1.9
- queries: bfloat16 [1024, 4096], P('ctx', 'tp'), may hold values from -87 to 87
- matchers: bfloat16 [1024, 4096], P('ctx', 'tp'), may hold values from -6 to 6
- segments: int32 [1024], replicated, may hold values from 0 to 3, never falling along the last dimension, each value on 1 to 768 neighbouring positions
- cotangent: bfloat16 [1024, 4096], P('ctx', 'tp'), may hold values from -6 to 6
Outputs:
- result: bfloat16 [1024, 4096], P('ctx', 'tp')
- stream_grad: bfloat16 [1024, 4096], P('ctx', 'tp')
- shutter_grad: bfloat16 [1024, 4096], P('ctx', 'tp')
- feeder_grad: bfloat16 [1024, 4096], P('ctx', 'tp')
- stencil_grad: float32 [7, 4096], P(None, 'tp')
- valves_grad: bfloat16 [1024, 4096], P('ctx', 'tp')
- intake_grad: bfloat16 [1024, 4096], P('ctx', 'tp')
- kernel_grad: float32 [128, 4096], P(None, 'tp')
- scaling_grad: float32 [4096], P('tp')
- queries_grad: bfloat16 [1024, 4096], P('ctx', 'tp')
- matchers_grad: bfloat16 [1024, 4096], P('ctx', 'tp')
Inputs may be any that keep to these rules, and one draw needn't show every extreme that they name: `segments`: document numbers never fall along the context; each of the 4 documents covers 1 to 768 positions, and one covers exactly 768.
All inputs are finite; a program needn't handle non-finite values.
Results may differ from a plain program's by a relative error of at most 0.03.
Values may be sent and summed in bfloat16 or wider, within the bound.
No kernel may reach another device: no remote copies, remote signals or barrier semaphores. Data moves between devices by JAX's collectives and lax.ppermute only.
A program may use at most 192 MiB of HBM per device.

v0:
```python
import math
import jax
import jax.numpy as jnp
from jax import lax
from jax.sharding import PartitionSpec as P

HD = 128
D = 4096
KS = 7
KM = 128
epsilon = 1e-06


def as_sent(shard):

    def short(part):
        return part.astype(jnp.bfloat16) if part.dtype == jnp.float32 else part

    return jax.tree.map(short, shard)


def passed_along(value, axis, steps):
    count = lax.axis_size(axis)
    leading, last = (max(0, -steps), min(count, count - steps))
    return lax.ppermute(value, axis, [(source, source + steps) for source in range(leading, last)])


def depthwise(padded, tap_rows):
    return lax.conv_general_dilated(
        padded[None],
        tap_rows[:, None, :],
        (1,),
        "VALID",
        dimension_numbers=("NWC", "WIO", "NWC"),
        feature_group_count=padded.shape[1],
        precision=lax.Precision.HIGHEST,
    )[0]


def neighbor_rows(edge_rows, offset):
    return passed_along(as_sent(edge_rows), "ctx", offset).astype(edge_rows.dtype)


def channel_total(partial_value):
    return lax.psum(partial_value, "tp")


def shards(
    stream,
    shutter,
    feeder,
    stencil,
    valves,
    intake,
    kernel,
    scaling,
    queries,
    matchers,
    segments,
    cotangent,
):
    local_rows = stream.shape[0]
    width_local = stream.shape[1]
    head_count = width_local // HD
    total_rows = local_rows * lax.axis_size("ctx")
    position = lax.axis_index("ctx") * local_rows
    scale_factor = 1.0 / math.sqrt(HD)
    widened = stream.astype(jnp.float32)
    inner_one = feeder.astype(jnp.float32) * widened
    rim_one = neighbor_rows(inner_one[local_rows - (KS - 1) :], 1)
    padded_one = jnp.concatenate([rim_one, inner_one], axis=0)
    conv_one = depthwise(padded_one, stencil[::-1])
    first_out = (widened + shutter.astype(jnp.float32) * conv_one).astype(jnp.bfloat16)
    first_wide = first_out.astype(jnp.float32)
    inner_two = intake.astype(jnp.float32) * first_wide
    rim_two = neighbor_rows(inner_two[local_rows - (KM - 1) :], 1)
    padded_two = jnp.concatenate([rim_two, inner_two], axis=0)
    conv_two = depthwise(padded_two, kernel[::-1])
    second_out = (first_wide + valves.astype(jnp.float32) * conv_two).astype(jnp.bfloat16)
    second_wide = second_out.astype(jnp.float32)
    squares = channel_total(jnp.sum(second_wide * second_wide, axis=1))
    inverse_rms = lax.rsqrt(squares / D + epsilon)
    normed = (second_wide * inverse_rms[:, None] * scaling).astype(jnp.bfloat16)
    keys_whole, values_whole = (
        lax.all_gather(matchers, "ctx", axis=0, tiled=True),
        lax.all_gather(normed, "ctx", axis=0, tiled=True),
    )
    query_pos = position + jnp.arange(local_rows, dtype=jnp.int32)
    key_pos = jnp.arange(total_rows, dtype=jnp.int32)
    query_seg = lax.dynamic_slice_in_dim(segments, position, local_rows, 0)
    visible = (key_pos[None, :] <= query_pos[:, None]) & (segments[None, :] == query_seg[:, None])
    contract = (((1,), (1,)), ((), ()))
    weight_list = []
    dscore_list = []
    attended_list = []
    query_grad_list = []
    logsum_list = []
    delta_list = []
    for head_index in range(head_count):
        columns = slice(head_index * HD, (head_index + 1) * HD)
        query_head = queries[:, columns]
        key_head = keys_whole[:, columns]
        value_head = values_whole[:, columns]
        cotangent_head = cotangent[:, columns]
        scores = (
            lax.dot_general(query_head, key_head, contract, preferred_element_type=jnp.float32)
            * scale_factor
        )
        scores = jnp.where(visible, scores, -jnp.inf)
        row_max = jnp.max(scores, axis=1)
        logsum = row_max + jnp.log(jnp.sum(jnp.exp(scores - row_max[:, None]), axis=1))
        weights = jnp.exp(scores - logsum[:, None]).astype(jnp.bfloat16)
        attended = jnp.dot(weights, value_head, preferred_element_type=jnp.float32)
        weight_grad = lax.dot_general(
            cotangent_head, value_head, contract, preferred_element_type=jnp.float32
        )
        row_delta = jnp.sum(cotangent_head.astype(jnp.float32) * attended, axis=1)
        dscore = (
            scale_factor * weights.astype(jnp.float32) * (weight_grad - row_delta[:, None])
        ).astype(jnp.bfloat16)
        query_grad = jnp.dot(dscore, key_head, preferred_element_type=jnp.float32)
        weight_list.append(weights)
        dscore_list.append(dscore)
        attended_list.append(attended)
        query_grad_list.append(query_grad)
        logsum_list.append(logsum)
        delta_list.append(row_delta)
    attended_all = jnp.concatenate(attended_list, axis=1)
    result = (second_wide + attended_all).astype(jnp.bfloat16)
    queries_grad = jnp.concatenate(query_grad_list, axis=1).astype(jnp.bfloat16)
    query_heads = queries.reshape(local_rows, head_count, HD)
    cotangent_heads = cotangent.reshape(local_rows, head_count, HD)
    weights_all = jnp.stack(weight_list)
    dscore_all = jnp.stack(dscore_list)
    dscore_part = lax.slice_in_dim(dscore_all, 0, local_rows * lax.axis_size("ctx"), axis=2)
    key_part = jnp.einsum(
        "hts,the->she", dscore_part, query_heads, preferred_element_type=jnp.float32
    )
    value_part = jnp.einsum(
        "hts,the->she", weights_all, cotangent_heads, preferred_element_type=jnp.float32
    )
    summed = lax.psum_scatter(
        jnp.concatenate(
            [
                key_part.reshape(local_rows * lax.axis_size("ctx"), width_local),
                value_part.reshape(local_rows * lax.axis_size("ctx"), width_local),
            ],
            axis=1,
        ).astype(jnp.bfloat16),
        "ctx",
        scatter_dimension=0,
        tiled=True,
    ).astype(jnp.float32)
    matchers_grad = summed[:, :width_local].astype(jnp.bfloat16)
    value_grad = summed[:, width_local:]
    gain_part = value_grad * scaling
    projected = channel_total(jnp.sum(gain_part * second_wide, axis=1))
    scaling_part = jnp.sum(value_grad * second_wide * inverse_rms[:, None], axis=0)
    second_grad = (
        cotangent.astype(jnp.float32)
        + inverse_rms[:, None] * gain_part
        - second_wide * (inverse_rms**3 * projected / D)[:, None]
    )
    valves_grad = (second_grad * conv_two).astype(jnp.bfloat16)
    dconv_two = second_grad * valves.astype(jnp.float32)
    back_two = neighbor_rows(dconv_two[: KM - 1], -1)
    dinner_two = depthwise(jnp.concatenate([dconv_two, back_two], axis=0), kernel)
    intake_grad = (dinner_two * first_wide).astype(jnp.bfloat16)
    kernel_part = depthwise(padded_two, dconv_two)[::-1]
    first_grad = second_grad + dinner_two * intake.astype(jnp.float32)
    shutter_grad = (first_grad * conv_one).astype(jnp.bfloat16)
    dconv_one = first_grad * shutter.astype(jnp.float32)
    back_one = neighbor_rows(dconv_one[: KS - 1], -1)
    dinner_one = depthwise(jnp.concatenate([dconv_one, back_one], axis=0), stencil)
    feeder_grad = (dinner_one * widened).astype(jnp.bfloat16)
    stencil_part = depthwise(padded_one, dconv_one)[::-1]
    stream_grad = (first_grad + dinner_one * feeder.astype(jnp.float32)).astype(jnp.bfloat16)
    stencil_sum, kernel_sum, scaling_sum = (
        lax.psum(stencil_part.astype(jnp.bfloat16), "ctx").astype(jnp.float32),
        lax.psum(kernel_part.astype(jnp.bfloat16), "ctx").astype(jnp.float32),
        lax.psum(scaling_part.astype(jnp.bfloat16), "ctx").astype(jnp.float32),
    )
    normalizer = math.sqrt(total_rows)
    return (
        result,
        stream_grad,
        shutter_grad,
        feeder_grad,
        stencil_sum / normalizer,
        valves_grad,
        intake_grad,
        kernel_sum / normalizer,
        scaling_sum / normalizer,
        queries_grad,
        matchers_grad,
    )


def solution(mesh):
    placed = (
        P("ctx", "tp"),
        P("ctx", "tp"),
        P("ctx", "tp"),
        P(None, "tp"),
        P("ctx", "tp"),
        P("ctx", "tp"),
        P(None, "tp"),
        P("tp"),
        P("ctx", "tp"),
        P("ctx", "tp"),
        P(),
        P("ctx", "tp"),
    )
    return jax.shard_map(
        shards,
        mesh=mesh,
        in_specs=placed,
        out_specs=(
            P("ctx", "tp"),
            P("ctx", "tp"),
            P("ctx", "tp"),
            P("ctx", "tp"),
            P(None, "tp"),
            P("ctx", "tp"),
            P("ctx", "tp"),
            P(None, "tp"),
            P("tp"),
            P("ctx", "tp"),
            P("ctx", "tp"),
        ),
        check_vma=False,
    )
```

profile of v0, /device:TPU:0, one launch (start us, length us, event | category | flops | bytes accessed | tf_op | source)
XLA Modules:
  0.0 272.9 jit_solution(10646670163490515569)
XLA Ops:
  9.1 2.4 collective-permute-start
  11.4 2.8 %rev.12 = f32[7,1024]{1,0:T(8,128)S(1)} reverse(f32[7,1024]{1,0:T(8,128)} %param.15), dimensions={0} | reverse | bytes 57344 | tf_op jit(solution)/shard_map/rev | solution.py:72
  18.3 4.5 %collective-permute-start.1 = (bf16[127,1024]{1,0:T(8,128)(2,1)}, bf16[127,1024]{1,0:T(8,128)(2,1)S(1)}, u32[]{:S(2)}, u32[]{:S(2)}) collective-permute-start(bf16[127,1024]{1,0:T(8,128)(2,1)} %slice.349), channel_id=1, source_target_pairs={{0,4},{4,8},{8,12},{12,16},{16,20},{20,24},{24,28},{1,5},{5,9},{9,... | collective-permute-start | bytes 780296 | tf_op jit(solution)/shard_map/ppermute | solution.py:25
  25.1 5.6 %fusion.74 = f32[1,128,1024]{2,0,1:T(1,128)S(1)} fusion(f32[1,255,1024]{2,0,1:T(1,128)S(1)} %broadcast_in_dim.33, f32[128,1,1024]{2,0,1:T(8,128)S(1)} %bitcast.165), kind=kOutput, calls=%fused_computation.133 | convolution fusion | flops 201326592 | bytes 2093056 | tf_op jit(solution)/shard_map/conv_general_dilated | solution.py:29
  31.6 11.9 %psum.35 = f32[128]{0:T(128)S(1)} all-reduce(f32[128]{0:T(128)S(1)} %get-tuple-element.63), channel_id=1, replica_groups=mesh['ctx'=8,'tp'=4] {'tp'}, use_global_device_ids=true, to_apply=%region_3.4 | all-reduce | flops 128 | bytes 1024 | tf_op jit(solution)/shard_map/psum | solution.py:45
  64.7 2.6 copy.116
  67.3 7.6 %all-gather.5.cloned.1.call-done = bf16[1024,1024]{1,0:T(8,128)(2,1)} async-done(((bf16[128,1024]{1,0:T(8,128)(2,1)}), bf16[1024,1024]{1,0:T(8,128)(2,1)}) %all-gather.5.cloned.1.call-update) | async-done | bytes 2097168 | tf_op jit(solution)/shard_map/all_gather | solution.py:86
  74.9 1.4 fusion.87
  91.7 2.6 copy.114
  94.3 4.7 %pad_maximum_fusion = bf16[1024,2048]{1,0:T(8,128)(2,1)} fusion(bf16[1024,1024]{1,0:T(8,128)(2,1)} %copy.116, bf16[1024,1024]{1,0:T(8,128)(2,1)} %copy.114), kind=kLoop, calls=%fused_computation | loop fusion | flops 8388608 | bytes 8388608 | tf_op jit(solution)/shard_map/concatenate | solution.py:143
  99.3 1.7 copy.68
  101.0 1.6 copy.67
  104.3 1.5 constant_dynamic-update-slice_fusion.7
  105.8 1.5 constant_dynamic-update-slice_fusion.6
  107.3 1.5 constant_dynamic-update-slice_fusion.5
  108.8 1.5 constant_dynamic-update-slice_fusion.4
  111.6 1.9 fusion.39
  113.5 1.9 fusion.38
  115.4 1.8 fusion.37
  117.2 1.8 fusion.36
  119.1 1.9 fusion.35
  120.9 1.9 fusion.34
  124.7 25.8 %reduce-scatter.2.cloned.1.call-done = bf16[128,2048]{1,0:T(8,128)(2,1)} async-done(((bf16[1024,2048]{1,0:T(8,128)(2,1)}), bf16[128,2048]{1,0:T(8,128)(2,1)}) %reduce-scatter.2.cloned.1.call-update) | async-done | bytes 524304 | tf_op jit(solution)/shard_map/reduce_scatter | solution.py:142
  151.7 11.7 %psum.36 = f32[128]{0:T(128)S(1)} all-reduce(f32[128]{0:T(128)S(1)} %get-tuple-element.34), channel_id=1, replica_groups=mesh['ctx'=8,'tp'=4] {'tp'}, use_global_device_ids=true, to_apply=%region_28.29 | all-reduce | flops 128 | bytes 1024 | tf_op jit(solution)/shard_map/psum | solution.py:45
  164.6 6.8 %fusion.70 = bf16[1,128,1024]{2,0,1:T(2,128)(2,1)S(1)} fusion(f32[1,255,1024]{2,0,1:T(1,128)} %copy-done.30, f32[128,1,1024]{2,0,1:T(8,128)S(1)} %bitcast.159), kind=kOutput, calls=%fused_computation.129 | convolution fusion | flops 201326592 | bytes 1830912 | tf_op jit(solution)/shard_map/conv_general_dilated | solution.py:29
  171.5 2.6 rev.15
  176.9 1.8 copy.104
  179.4 45.7 %all-reduce.3.cloned.1.call-done = bf16[128,1024]{1,0:T(8,128)(2,1)} async-done(((bf16[128,1024]{1,0:T(8,128)(2,1)}), bf16[128,1024]{1,0:T(8,128)(2,1)}) %all-reduce.3.cloned.1.call-update) | async-done | bytes 262160 | tf_op jit(solution)/shard_map/psum | solution.py:180
  225.1 1.8 convert_multiply_fusion.16
  227.1 5.8 %fusion.40 = f32[1,128,1024]{2,0,1:T(1,128)S(1)} fusion(f32[1,255,1024]{2,1,0:T(8,128)S(1)} %maximum_bitcast_fusion, f32[128,1,1024]{2,0,1:T(8,128)S(1)} %bitcast.164), kind=kOutput, calls=%fused_computation.77 | convolution fusion | flops 201326592 | bytes 2093056 | tf_op jit(solution)/shard_map/conv_general_dilated | solution.py:29
  232.9 2.7 %multiply_convert_fusion = (bf16[128,1024]{1,0:T(8,128)(2,1)}, f32[128,1024]{1,0:T(8,128)S(1)}, bf16[128,1024]{1,0:T(8,128)(2,1)}, bf16[128,1024]{1,0:T(8,128)(2,1)}, bf16[128,1024]{1,0:T(8,128)(2,1)}) fusion(f32[1,136,1024]{2,1,0:T(8,128)S(1)} %reshape.119, bf16[128,1024]{1,0:T(8,128)(2,1)S(1)} %copy-done.26, f32[1,128,1024]{2,0,1:T(1,128)S(1)} %fusion.40, ...), kind=kLoop, calls=%fused_computation.136 | loop fusion | flops 2621440 | bytes 4985856 | tf_op jit(solution)/shard_map/convert_element_type | solution.py:171
  237.1 22.4 %all-reduce = (bf16[7,1024]{1,0:T(8,128)(2,1)S(1)}, bf16[1024]{0:T(1024)(128)(2,1)S(1)}) all-reduce(bf16[7,1024]{1,0:T(8,128)(2,1)S(1)} %rev.14, bf16[1024]{0:T(1024)(128)(2,1)S(1)} %get-tuple-element.33), channel_id=1, replica_groups=mesh['ctx'=8,'tp'=4] {'ctx'}, use_global_device_ids=true, to_apply=%region_29.30 | all-reduce | flops 8192 | bytes 32768 | tf_op jit(solution)/shard_map/psum | solution.py:179
  (207 shorter events, 64.4 us)
Async XLA Ops:
  7.2 37.5 %all-gather.3.cloned.1.call-start = ((), (), s32[]{:S(2)}) async-start(), calls=%async_computation.1 | async-start | bytes 2359296 | tf_op jit(solution)/shard_map/all_gather | solution.py:85
  7.9 67.0 %all-gather.5.cloned.1.call-start = ((), (), s32[]{:S(2)}) async-start(), calls=%async_computation.2 | async-start | bytes 2359296 | tf_op jit(solution)/shard_map/all_gather | solution.py:86
  9.1 5.2 %collective-permute-start = (bf16[6,1024]{1,0:T(8,128)(2,1)S(1)}, bf16[6,1024]{1,0:T(8,128)(2,1)S(1)}, u32[]{:S(2)}, u32[]{:S(2)}) collective-permute-start(bf16[6,1024]{1,0:T(8,128)(2,1)S(1)} %slice.351), channel_id=1, source_target_pairs={{0,4},{4,8},{8,12},{12,16},{16,20},{20,24},{24,28},{1,5},{5,9},{9,... | collective-permute-start | bytes 36872 | tf_op jit(solution)/shard_map/ppermute | solution.py:25
  16.6 6.2 %copy-start.33 = (f32[128,1024]{1,0:T(8,128)S(1)}, f32[128,1024]{1,0:T(8,128)}, u32[]{:S(2)}) copy-start(f32[128,1024]{1,0:T(8,128)} %param.18) | copy-start | bytes 1572868
  17.4 5.8 %copy-start.1 = (bf16[128,1024]{1,0:T(8,128)(2,1)S(1)}, bf16[128,1024]{1,0:T(8,128)(2,1)}, u32[]{:S(2)}) copy-start(bf16[128,1024]{1,0:T(8,128)(2,1)} %param.23) | copy-start | bytes 786436
  17.4 5.9 %copy-start.36 = (bf16[128,1024]{1,0:T(8,128)(2,1)S(1)}, bf16[128,1024]{1,0:T(8,128)(2,1)}, u32[]{:S(2)}) copy-start(bf16[128,1024]{1,0:T(8,128)(2,1)} %param.20) | copy-start | bytes 786436
  17.4 6.8 %copy-start.39 = (s32[1024]{0:T(1024)S(1)}, s32[1024]{0:T(1024)}, u32[]{:S(2)}) copy-start(s32[1024]{0:T(1024)} %param.22) | copy-start | bytes 12292
  17.5 13.3 %copy-start.2 = (bf16[128,1024]{1,0:T(8,128)(2,1)}, bf16[128,1024]{1,0:T(8,128)(2,1)S(1)}, u32[]{:S(2)}) copy-start(bf16[128,1024]{1,0:T(8,128)(2,1)S(1)} %get-tuple-element.66) | copy-start | bytes 786436
  18.3 5.9 %collective-permute-start.1 = (bf16[127,1024]{1,0:T(8,128)(2,1)}, bf16[127,1024]{1,0:T(8,128)(2,1)S(1)}, u32[]{:S(2)}, u32[]{:S(2)}) collective-permute-start(bf16[127,1024]{1,0:T(8,128)(2,1)} %slice.349), channel_id=1, source_target_pairs={{0,4},{4,8},{8,12},{12,16},{16,20},{20,24},{24,28},{1,5},{5,9},{9,... | collective-permute-start | bytes 780296 | tf_op jit(solution)/shard_map/ppermute | solution.py:25
  25.1 5.7 %copy-start.30 = (f32[1,255,1024]{2,0,1:T(1,128)}, f32[1,255,1024]{2,0,1:T(1,128)S(1)}, u32[]{:S(2)}) copy-start(f32[1,255,1024]{2,0,1:T(1,128)S(1)} %broadcast_in_dim.33) | copy-start | bytes 3133444
  25.1 5.7 %copy-start.20 = (bf16[128,1024]{1,0:T(8,128)(2,1)S(1)}, bf16[128,1024]{1,0:T(8,128)(2,1)}, u32[]{:S(2)}) copy-start(bf16[128,1024]{1,0:T(8,128)(2,1)} %param.16) | copy-start | bytes 786436
  25.1 18.4 %copy-start.37 = (f32[1024]{0:T(1024)S(1)}, f32[1024]{0:T(1024)}, u32[]{:S(2)}) copy-start(f32[1024]{0:T(1024)} %param.19) | copy-start | bytes 12292
  44.4 106.1 %reduce-scatter.2.cloned.1.call-start = ((), (), s32[]{:S(2)}) async-start(), calls=%async_computation.3 | async-start | bytes 4718592 | tf_op jit(solution)/shard_map/reduce_scatter | solution.py:142
  67.3 14.2 %copy-start.4 = (bf16[128,1024]{1,0:T(8,128)(2,1)S(1)}, bf16[128,1024]{1,0:T(8,128)(2,1)}, u32[]{:S(2)}) copy-start(bf16[128,1024]{1,0:T(8,128)(2,1)} %get-tuple-element.60) | copy-start | bytes 786436
  74.9 5.4 %copy-start = (bf16[1024,1024]{1,0:T(8,128)(2,1)S(1)}, bf16[1024,1024]{1,0:T(8,128)(2,1)}, u32[]{:S(2)}) copy-start(bf16[1024,1024]{1,0:T(8,128)(2,1)} %all-gather.5.cloned.1.call-done) | copy-start | bytes 6291460
  74.9 6.9 %copy-start.24 = (bf16[128,1024]{1,0:T(8,128)(2,1)S(1)}, bf16[128,1024]{1,0:T(8,128)(2,1)}, u32[]{:S(2)}) copy-start(bf16[128,1024]{1,0:T(8,128)(2,1)} %get-tuple-element.62) | copy-start | bytes 786436
  74.9 7.3 %copy-start.10 = (bf16[128,1024]{1,0:T(8,128)(2,1)S(1)}, bf16[128,1024]{1,0:T(8,128)(2,1)}, u32[]{:S(2)}) copy-start(bf16[128,1024]{1,0:T(8,128)(2,1)} %get-tuple-element.48) | copy-start | bytes 786436
  83.1 3.9 %copy-start.7 = (bf16[128,1024]{1,0:T(8,128)(2,1)S(1)}, bf16[128,1024]{1,0:T(8,128)(2,1)}, u32[]{:S(2)}) copy-start(bf16[128,1024]{1,0:T(8,128)(2,1)} %get-tuple-element.54) | copy-start | bytes 786436
  84.1 3.9 %copy-start.8 = (bf16[128,1024]{1,0:T(8,128)(2,1)S(1)}, bf16[128,1024]{1,0:T(8,128)(2,1)}, u32[]{:S(2)}) copy-start(bf16[128,1024]{1,0:T(8,128)(2,1)} %get-tuple-element.52) | copy-start | bytes 786436
  99.0 12.6 %copy-start.17 = (bf16[1024,1024]{1,0:T(8,128)(2,1)S(1)}, bf16[1024,1024]{1,0:T(8,128)(2,1)}, u32[]{:S(2)}) copy-start(bf16[1024,1024]{1,0:T(8,128)(2,1)} %all-gather.3.cloned.1.call-done) | copy-start | bytes 6291460
  99.0 126.1 %all-reduce.3.cloned.1.call-start = ((), (), s32[]{:S(2)}) async-start(), calls=%async_computation.4 | async-start | bytes 524288 | tf_op jit(solution)/shard_map/psum | solution.py:180
  104.3 18.6 %copy-start.22 = (bf16[128,1024]{1,0:T(8,128)(2,1)S(1)}, bf16[128,1024]{1,0:T(8,128)(2,1)}, u32[]{:S(2)}) copy-start(bf16[128,1024]{1,0:T(8,128)(2,1)} %get-tuple-element.102) | copy-start | bytes 786436
  110.3 13.4 %copy-start.23 = (bf16[128,1024]{1,0:T(8,128)(2,1)S(1)}, bf16[128,1024]{1,0:T(8,128)(2,1)}, u32[]{:S(2)}) copy-start(bf16[128,1024]{1,0:T(8,128)(2,1)} %get-tuple-element.104) | copy-start | bytes 786436
  113.5 49.9 %copy-start.21 = (bf16[128,1024]{1,0:T(8,128)(2,1)S(1)}, bf16[128,1024]{1,0:T(8,128)(2,1)}, u32[]{:S(2)}) copy-start(bf16[128,1024]{1,0:T(8,128)(2,1)} %param.16) | copy-start | bytes 786436
  164.6 10.2 %copy-start.35 = (f32[128,128]{0,1:T(8,128)S(1)}, f32[128,128]{0,1:T(8,128)}, u32[]{:S(2)}) copy-start(f32[128,128]{0,1:T(8,128)} %get-tuple-element.88) | copy-start | bytes 196612
  171.4 7.2 %copy-start.18 = (bf16[128,2048]{1,0:T(8,128)(2,1)S(1)}, bf16[128,2048]{1,0:T(8,128)(2,1)}, u32[]{:S(2)}) copy-start(bf16[128,2048]{1,0:T(8,128)(2,1)} %reduce-scatter.2.cloned.1.call-done) | copy-start | bytes 1572868
  174.9 51.9 %collective-permute-start.2 = (bf16[127,1024]{1,0:T(8,128)(2,1)S(1)}, bf16[127,1024]{1,0:T(8,128)(2,1)S(1)}, u32[]{:S(2)}, u32[]{:S(2)}) collective-permute-start(bf16[127,1024]{1,0:T(8,128)(2,1)S(1)} %slice.348), channel_id=1, source_target_pairs={{4,0},{8,4},{12,8},{16,12},{20,16},{24,20},{28,24},{5,1},{9,5},{13... | collective-permute-start | bytes 780296 | tf_op jit(solution)/shard_map/ppermute | solution.py:25
  178.7 48.4 %copy-start.34 = (f32[128,1024]{1,0:T(8,128)S(1)}, f32[128,1024]{1,0:T(8,128)}, u32[]{:S(2)}) copy-start(f32[128,1024]{1,0:T(8,128)} %param.18) | copy-start | bytes 1572868
  227.0 5.8 %copy-start.3 = (bf16[128,1024]{1,0:T(8,128)(2,1)S(1)}, bf16[128,1024]{1,0:T(8,128)(2,1)}, u32[]{:S(2)}) copy-start(bf16[128,1024]{1,0:T(8,128)(2,1)} %copy-done.2) | copy-start | bytes 786436
  227.1 5.8 %copy-start.16 = (f32[1,128,1024]{2,0,1:T(1,128)S(1)}, f32[1,128,1024]{2,0,1:T(1,128)}, u32[]{:S(2)}) copy-start(f32[1,128,1024]{2,0,1:T(1,128)} %copy-done.15) | copy-start | bytes 1572868
  227.1 5.8 %copy-start.26 = (bf16[128,1024]{1,0:T(8,128)(2,1)S(1)}, bf16[128,1024]{1,0:T(8,128)(2,1)}, u32[]{:S(2)}) copy-start(bf16[128,1024]{1,0:T(8,128)(2,1)} %param.17) | copy-start | bytes 786436
  260.1 3.1 %collective-permute-start.3 = (bf16[6,1024]{1,0:T(8,128)(2,1)S(1)}, bf16[6,1024]{1,0:T(8,128)(2,1)S(1)}, u32[]{:S(2)}, u32[]{:S(2)}) collective-permute-start(bf16[6,1024]{1,0:T(8,128)(2,1)S(1)} %slice.350), channel_id=1, source_target_pairs={{4,0},{8,4},{12,8},{16,12},{20,16},{24,20},{28,24},{5,1},{9,5},{13... | collective-permute-start | bytes 36872 | tf_op jit(solution)/shard_map/ppermute | solution.py:25
  (17 other events, 31.2 us)
Sparse Core Ops, SparseCore 0:
  9.9 30.5 all-gather.2
  44.5 30.3 all-gather.4
  99.1 51.3 reduce-scatter.1
  174.3 50.7 all-reduce.2
where the time goes:
time: 274 us; the launch traced here: 273 us
  waiting for transfers between devices  81 us (30%)
  matrix products  60.8 us (22%)
  blocking collectives  46 us (17%)
  local copies, waits for them, and re-layouts  35.2 us (13%)
  other arithmetic  25.2 us (9%)
  between operations  14.6 us (5%)
  starting transfers between devices  10 us (4%)
    psum x1, waiting for transfers between devices, shards(): lax.psum(kernel_part.astype(jnp.bfloat16), 'ctx').astype(jnp.float32)  45.7 us
    reduce_scatter x1, waiting for transfers between devices, shards(): lax.psum_scatter(jnp.concatenate([key_part.reshape(local_rows * lax.axis_...  25.8 us
    psum x2, blocking collectives, channel_total(): return lax.psum(partial_value, 'tp')  23.6 us
    psum x1, blocking collectives, shards(): lax.psum(stencil_part.astype(jnp.bfloat16), 'ctx').astype(jnp.float32)  22.4 us
    conv_general_dilated x6, matrix products, depthwise(): lax.conv_general_dilated(padded[None], tap_rows[:, None, :], (1,), 'VALID...  19.9 us
    dot_general x8, matrix products, shards(): query_grad = jnp.dot(dscore, key_head, preferred_element_type=jnp.float32)  13 us
    unnamed x93, local copies, waits for them, and re-layouts  12.7 us
    dot_general x8, matrix products, shards(): lax.dot_general(query_head, key_head, contract, preferred_element_type=jn...  10.6 us
  transfers between devices with their start and end apart: 8, of which 4 were waited for; matrix products, arithmetic and copies ran while one was open for 25% of the time, Pallas kernels for 0%

commit v1 on v0

--- a/solution.py
+++ b/solution.py
@@ -81,9 +81,24 @@
     squares = channel_total(jnp.sum(second_wide * second_wide, axis=1))
     inverse_rms = lax.rsqrt(squares / D + epsilon)
     normed = (second_wide * inverse_rms[:, None] * scaling).astype(jnp.bfloat16)
+
+    def carry_bands(view, bus_axis):
+        item_now, vec_out = (lax.axis_size(bus_axis), lax.axis_index(bus_axis))
+        reply, e_next = (view, 1)
+        while e_next < item_now:
+            sheets = []
+            for ix in range(item_now):
+                sheets.append((ix, ix ^ e_next))
+            new = lax.ppermute(reply, bus_axis, sheets)
+            mat_out = jnp.concatenate([reply, new], axis=0)
+            outer = jnp.concatenate([new, reply], axis=0)
+            reply = jnp.where(vec_out & e_next == 0, mat_out, outer)
+            e_next = 2 * e_next
+        return reply
+
     keys_whole, values_whole = (
         lax.all_gather(matchers, "ctx", axis=0, tiled=True),
-        lax.all_gather(normed, "ctx", axis=0, tiled=True),
+        carry_bands(normed, bus_axis="ctx"),
     )
     query_pos = position + jnp.arange(local_rows, dtype=jnp.int32)
     key_pos = jnp.arange(total_rows, dtype=jnp.int32)

time: 274 us -> 304 us (1.11)
  waiting for transfers between devices: 81 us -> 107 us
  starting transfers between devices: 10 us -> 18.6 us
    ppermute x0 -> x3, waiting for transfers between devices: none -> 34.1 us  [carry_bands(): new = lax.ppermute(reply, bus_axis, sheets)]
    ppermute x0 -> x3, starting transfers between devices: none -> 8.99 us  [carry_bands(): new = lax.ppermute(reply, bus_axis, sheets)]
    all_gather x1 -> x0, waiting for transfers between devices: 7.58 us -> none  [shards(): lax.all_gather(normed, 'ctx', axis=0, tiled=True)]
    unnamed x7, other arithmetic: 5.92 us -> 1.02 us
    dot_general x8, matrix products: 8.07 us -> 3.21 us  [shards(): attended = jnp.dot(weights, value_head, preferred_element_type=jnp.float32)]
    select_n x0 -> x3, other arithmetic: none -> 3.95 us  [carry_bands(): reply = jnp.where(vec_out & e_next == 0, mat_out, outer)]
    unnamed x93 -> x95, local copies, waits for them, and re-layouts: 12.7 us -> 11.9 us
  transfers between devices with their start and end apart: 8 -> 10, of which waited for: 4 -> 7; matrix products, arithmetic and copies ran while one was open for 25% -> 15% of each run, Pallas kernels for 0% -> 0%
where the time goes in v1:
time: 304 us; the launch traced here: 302 us
  waiting for transfers between devices  107 us (35%)
  matrix products  58.7 us (19%)
  blocking collectives  46.3 us (15%)
  local copies, waits for them, and re-layouts  34.5 us (11%)
  other arithmetic  22.8 us (8%)
  starting transfers between devices  18.6 us (6%)
  between operations  14.8 us (5%)
    psum x1, waiting for transfers between devices, shards(): lax.psum(kernel_part.astype(jnp.bfloat16), 'ctx').astype(jnp.float32)  45.7 us
    ppermute x3, waiting for transfers between devices, carry_bands(): new = lax.ppermute(reply, bus_axis, sheets)  34.1 us
    reduce_scatter x1, waiting for transfers between devices, shards(): lax.psum_scatter(jnp.concatenate([key_part.reshape(local_rows * lax.axis_...  24.9 us
    psum x2, blocking collectives, channel_total(): return lax.psum(partial_value, 'tp')  23.9 us
    psum x1, blocking collectives, shards(): lax.psum(stencil_part.astype(jnp.bfloat16), 'ctx').astype(jnp.float32)  22.4 us
    conv_general_dilated x6, matrix products, depthwise(): lax.conv_general_dilated(padded[None], tap_rows[:, None, :], (1,), 'VALID...  21.1 us
    dot_general x8, matrix products, shards(): query_grad = jnp.dot(dscore, key_head, preferred_element_type=jnp.float32)  13 us
    unnamed x95, local copies, waits for them, and re-layouts  11.9 us
  transfers between devices with their start and end apart: 10, of which 7 were waited for; matrix products, arithmetic and copies ran while one was open for 15% of the time, Pallas kernels for 0%

profile of v1, /device:TPU:0, one launch (start us, length us, event | category | flops | bytes accessed | tf_op | source)
XLA Modules:
  0.0 302.3 jit_solution(16478012472475460625)
XLA Ops:
  8.3 2.4 collective-permute-start
  10.7 2.8 rev.12
  16.8 4.5 %collective-permute-start.1 = (bf16[127,1024]{1,0:T(8,128)(2,1)S(1)}, bf16[127,1024]{1,0:T(8,128)(2,1)S(1)}, u32[]{:S(2)}, u32[]{:S(2)}) collective-permute-start(bf16[127,1024]{1,0:T(8,128)(2,1)S(1)} %slice.349), channel_id=1, source_target_pairs={{0,4},{4,8},{8,12},{12,16},{16,20},{20,24},{24,28},{1,5},{5,9},{9,... | collective-permute-start | bytes 780296 | tf_op jit(solution)/shard_map/ppermute | solution.py:25
  23.4 5.6 %fusion.74 = f32[1,128,1024]{2,0,1:T(1,128)S(1)} fusion(f32[1,255,1024]{2,0,1:T(1,128)S(1)} %broadcast_in_dim.33, f32[128,1,1024]{2,0,1:T(8,128)S(1)} %bitcast.165), kind=kOutput, calls=%fused_computation.136 | convolution fusion | flops 201326592 | bytes 2093056 | tf_op jit(solution)/shard_map/conv_general_dilated | solution.py:29
  29.9 12.2 %psum.35 = f32[128]{0:T(128)S(1)} all-reduce(f32[128]{0:T(128)S(1)} %get-tuple-element.63), channel_id=1, replica_groups=mesh['ctx'=8,'tp'=4] {'tp'}, use_global_device_ids=true, to_apply=%region_3.4 | all-reduce | flops 128 | bytes 1024 | tf_op jit(solution)/shard_map/psum | solution.py:45
  44.1 4.8 %collective-permute-start.3 = (bf16[256,1024]{1,0:T(8,128)(2,1)S(1)}, bf16[256,1024]{1,0:T(8,128)(2,1)S(1)}, u32[]{:S(2)}, u32[]{:S(2)}) collective-permute-start(bf16[256,1024]{1,0:T(8,128)(2,1)S(1)} %maximum_select_fusion.2), channel_id=1, source_target_pairs={{0,8},{4,12},{8,0},{12,4},{16,24},{20,28},{24,16},{28,20},{1,9},{5... | collective-permute-start | bytes 1572872 | tf_op jit(solution)/shard_map/ppermute | solution.py:92
  48.9 12.2 %collective-permute-done.3 = bf16[256,1024]{1,0:T(8,128)(2,1)S(1)} collective-permute-done((bf16[256,1024]{1,0:T(8,128)(2,1)S(1)}, bf16[256,1024]{1,0:T(8,128)(2,1)S(1)}, u32[]{:S(2)}, u32[]{:S(2)}) %collective-permute-start.3) | collective-permute-done | bytes 524320 | tf_op jit(solution)/shard_map/ppermute | solution.py:92
  61.6 3.6 %collective-permute-start.4 = (bf16[512,1024]{1,0:T(8,128)(2,1)S(1)}, bf16[512,1024]{1,0:T(8,128)(2,1)}, u32[]{:S(2)}, u32[]{:S(2)}) collective-permute-start(bf16[512,1024]{1,0:T(8,128)(2,1)S(1)} %maximum_select_fusion.1), channel_id=1, source_target_pairs={{0,16},{4,20},{8,24},{12,28},{16,0},{20,4},{24,8},{28,12},{1,17},{... | collective-permute-start | bytes 3145736 | tf_op jit(solution)/shard_map/ppermute | solution.py:92
  65.4 1.8 copy.113
  67.3 20.7 %collective-permute-done.4 = bf16[512,1024]{1,0:T(8,128)(2,1)} collective-permute-done((bf16[512,1024]{1,0:T(8,128)(2,1)S(1)}, bf16[512,1024]{1,0:T(8,128)(2,1)}, u32[]{:S(2)}, u32[]{:S(2)}) %collective-permute-start.4) | collective-permute-done | bytes 1048608 | tf_op jit(solution)/shard_map/ppermute | solution.py:92
  88.0 3.3 %maximum_select_fusion = bf16[1024,1024]{1,0:T(8,128)(2,1)S(1)} fusion(bf16[512,1024]{1,0:T(8,128)(2,1)} %collective-permute-done.4, bf16[512,1024]{1,0:T(8,128)(2,1)} %copy-done, pred[]{:T(512)S(6)} %eq.25), kind=kLoop, calls=%fused_computation.1 | loop fusion | flops 9437184 | bytes 4194305 | tf_op jit(solution)/shard_map/jit(_where)/select_n | solution.py:95
  117.1 2.6 copy.114
  119.7 2.3 convolution_convert_fusion
  122.0 2.6 copy.116
  124.6 4.7 %pad_maximum_fusion = bf16[1024,2048]{1,0:T(8,128)(2,1)} fusion(bf16[1024,1024]{1,0:T(8,128)(2,1)} %copy.116, bf16[1024,1024]{1,0:T(8,128)(2,1)} %copy.114), kind=kLoop, calls=%fused_computation | loop fusion | flops 8388608 | bytes 8388608 | tf_op jit(solution)/shard_map/concatenate | solution.py:158
  129.4 1.7 copy.67
  140.8 1.9 fusion.39
  142.7 1.9 fusion.38
  144.6 1.8 fusion.37
  146.4 1.8 fusion.36
  148.3 1.8 fusion.35
  150.1 1.9 fusion.34
  153.8 24.9 %reduce-scatter.2.cloned.1.call-done = bf16[128,2048]{1,0:T(8,128)(2,1)} async-done(((bf16[1024,2048]{1,0:T(8,128)(2,1)}), bf16[128,2048]{1,0:T(8,128)(2,1)}) %reduce-scatter.2.cloned.1.call-update) | async-done | bytes 524304 | tf_op jit(solution)/shard_map/reduce_scatter | solution.py:157
  179.8 11.7 %psum.36 = f32[128]{0:T(128)S(1)} all-reduce(f32[128]{0:T(128)S(1)} %get-tuple-element.34), channel_id=1, replica_groups=mesh['ctx'=8,'tp'=4] {'tp'}, use_global_device_ids=true, to_apply=%region_28.29 | all-reduce | flops 128 | bytes 1024 | tf_op jit(solution)/shard_map/psum | solution.py:45
  192.8 6.8 %fusion.70 = bf16[1,128,1024]{2,0,1:T(2,128)(2,1)S(1)} fusion(f32[1,255,1024]{2,0,1:T(1,128)} %copy-done.24, f32[128,1,1024]{2,0,1:T(8,128)S(1)} %bitcast.159), kind=kOutput, calls=%fused_computation.132 | convolution fusion | flops 201326592 | bytes 1830912 | tf_op jit(solution)/shard_map/conv_general_dilated | solution.py:29
  199.8 2.6 rev.15
  205.1 1.8 copy.104
  207.6 45.7 %all-reduce.3.cloned.1.call-done = bf16[128,1024]{1,0:T(8,128)(2,1)} async-done(((bf16[128,1024]{1,0:T(8,128)(2,1)}), bf16[128,1024]{1,0:T(8,128)(2,1)}) %all-reduce.3.cloned.1.call-update) | async-done | bytes 262160 | tf_op jit(solution)/shard_map/psum | solution.py:195
  253.3 1.8 convert_multiply_fusion.16
  255.3 7.0 %fusion.40 = f32[1,128,1024]{2,0,1:T(1,128)S(1)} fusion(f32[1,255,1024]{2,1,0:T(8,128)S(1)} %maximum_bitcast_fusion, f32[128,1,1024]{2,0,1:T(8,128)} %bitcast.164), kind=kOutput, calls=%fused_computation.79 | convolution fusion | flops 201326592 | bytes 2093056 | tf_op jit(solution)/shard_map/conv_general_dilated | solution.py:29
  262.4 2.7 multiply_convert_fusion
  266.6 22.4 %all-reduce = (bf16[7,1024]{1,0:T(8,128)(2,1)S(1)}, bf16[1024]{0:T(1024)(128)(2,1)S(1)}) all-reduce(bf16[7,1024]{1,0:T(8,128)(2,1)S(1)} %rev.14, bf16[1024]{0:T(1024)(128)(2,1)S(1)} %get-tuple-element.33), channel_id=1, replica_groups=mesh['ctx'=8,'tp'=4] {'ctx'}, use_global_device_ids=true, to_apply=%region_29.30 | all-reduce | flops 8192 | bytes 32768 | tf_op jit(solution)/shard_map/psum | solution.py:194
  (215 shorter events, 61.1 us)
Async XLA Ops:
  7.2 84.2 %all-gather.2.cloned.1.call-start = ((), (), s32[]{:S(2)}) async-start(), calls=%async_computation.1 | async-start | bytes 2359296 | tf_op jit(solution)/shard_map/all_gather | solution.py:100
  8.3 5.2 %collective-permute-start = (bf16[6,1024]{1,0:T(8,128)(2,1)S(1)}, bf16[6,1024]{1,0:T(8,128)(2,1)S(1)}, u32[]{:S(2)}, u32[]{:S(2)}) collective-permute-start(bf16[6,1024]{1,0:T(8,128)(2,1)S(1)} %slice.351), channel_id=1, source_target_pairs={{0,4},{4,8},{8,12},{12,16},{16,20},{20,24},{24,28},{1,5},{5,9},{9,... | collective-permute-start | bytes 36872 | tf_op jit(solution)/shard_map/ppermute | solution.py:25
  15.9 5.6 %copy-start.35 = (f32[128,1024]{1,0:T(8,128)S(1)}, f32[128,1024]{1,0:T(8,128)}, u32[]{:S(2)}) copy-start(f32[128,1024]{1,0:T(8,128)} %param.18) | copy-start | bytes 1572868
  16.8 12.3 %copy-start.3 = (bf16[128,1024]{1,0:T(8,128)(2,1)}, bf16[128,1024]{1,0:T(8,128)(2,1)S(1)}, u32[]{:S(2)}) copy-start(bf16[128,1024]{1,0:T(8,128)(2,1)S(1)} %get-tuple-element.66) | copy-start | bytes 786436
  16.8 5.7 %collective-permute-start.1 = (bf16[127,1024]{1,0:T(8,128)(2,1)S(1)}, bf16[127,1024]{1,0:T(8,128)(2,1)S(1)}, u32[]{:S(2)}, u32[]{:S(2)}) collective-permute-start(bf16[127,1024]{1,0:T(8,128)(2,1)S(1)} %slice.349), channel_id=1, source_target_pairs={{0,4},{4,8},{8,12},{12,16},{16,20},{20,24},{24,28},{1,5},{5,9},{9,... | collective-permute-start | bytes 780296 | tf_op jit(solution)/shard_map/ppermute | solution.py:25
  21.4 157.3 %reduce-scatter.2.cloned.1.call-start = ((), (), s32[]{:S(2)}) async-start(), calls=%async_computation.2 | async-start | bytes 4718592 | tf_op jit(solution)/shard_map/reduce_scatter | solution.py:157
  23.4 5.7 %copy-start.24 = (f32[1,255,1024]{2,0,1:T(1,128)}, f32[1,255,1024]{2,0,1:T(1,128)S(1)}, u32[]{:S(2)}) copy-start(f32[1,255,1024]{2,0,1:T(1,128)S(1)} %broadcast_in_dim.33) | copy-start | bytes 3133444
  23.4 5.7 %copy-start.15 = (bf16[128,1024]{1,0:T(8,128)(2,1)S(1)}, bf16[128,1024]{1,0:T(8,128)(2,1)}, u32[]{:S(2)}) copy-start(bf16[128,1024]{1,0:T(8,128)(2,1)} %param.16) | copy-start | bytes 786436
  23.4 18.7 %copy-start.38 = (f32[1024]{0:T(1024)S(1)}, f32[1024]{0:T(1024)}, u32[]{:S(2)}) copy-start(f32[1024]{0:T(1024)} %param.19) | copy-start | bytes 12292
  29.9 35.4 %copy-start.2 = (bf16[128,1024]{1,0:T(8,128)(2,1)S(1)}, bf16[128,1024]{1,0:T(8,128)(2,1)}, u32[]{:S(2)}) copy-start(bf16[128,1024]{1,0:T(8,128)(2,1)} %param.23) | copy-start | bytes 786436
  42.2 1.7 collective-permute-start.2
  42.8 24.4 %copy-start.40 = (s32[1024]{0:T(1024)S(1)}, s32[1024]{0:T(1024)}, u32[]{:S(2)}) copy-start(s32[1024]{0:T(1024)} %param.22) | copy-start | bytes 12292
  44.1 17.0 %collective-permute-start.3 = (bf16[256,1024]{1,0:T(8,128)(2,1)S(1)}, bf16[256,1024]{1,0:T(8,128)(2,1)S(1)}, u32[]{:S(2)}, u32[]{:S(2)}) collective-permute-start(bf16[256,1024]{1,0:T(8,128)(2,1)S(1)} %maximum_select_fusion.2), channel_id=1, source_target_pairs={{0,8},{4,12},{8,0},{12,4},{16,24},{20,28},{24,16},{28,20},{1,9},{5... | collective-permute-start | bytes 1572872 | tf_op jit(solution)/shard_map/ppermute | solution.py:92
  61.6 5.7 %copy-start = (bf16[512,1024]{1,0:T(8,128)(2,1)}, bf16[512,1024]{1,0:T(8,128)(2,1)S(1)}, u32[]{:S(2)}) copy-start(bf16[512,1024]{1,0:T(8,128)(2,1)S(1)} %maximum_select_fusion.1) | copy-start | bytes 3145732
  61.6 26.4 %collective-permute-start.4 = (bf16[512,1024]{1,0:T(8,128)(2,1)S(1)}, bf16[512,1024]{1,0:T(8,128)(2,1)}, u32[]{:S(2)}, u32[]{:S(2)}) collective-permute-start(bf16[512,1024]{1,0:T(8,128)(2,1)S(1)} %maximum_select_fusion.1), channel_id=1, source_target_pairs={{0,16},{4,20},{8,24},{12,28},{16,0},{20,4},{24,8},{28,12},{1,17},{... | collective-permute-start | bytes 3145736 | tf_op jit(solution)/shard_map/ppermute | solution.py:92
  107.3 4.2 %copy-start.1 = (bf16[8,128,1024]{2,1,0:T(8,128)(2,1)}, bf16[8,128,1024]{2,1,0:T(8,128)(2,1)S(1)}, u32[]{:S(2)}) copy-start(bf16[8,128,1024]{2,1,0:T(8,128)(2,1)S(1)} %get-tuple-element.47) | copy-start | bytes 6291460
  129.3 4.2 %copy-start.28 = (f32[128,128]{0,1:T(8,128)S(1)}, f32[128,128]{0,1:T(8,128)}, u32[]{:S(2)}) copy-start(f32[128,128]{0,1:T(8,128)} %copy-done.27) | copy-start | bytes 196612
  129.3 4.3 %copy-start.26 = (f32[128,128]{0,1:T(8,128)S(1)}, f32[128,128]{0,1:T(8,128)}, u32[]{:S(2)}) copy-start(f32[128,128]{0,1:T(8,128)} %copy-done.25) | copy-start | bytes 196612
  129.3 11.6 %copy-start.11 = (bf16[1024,1024]{1,0:T(8,128)(2,1)S(1)}, bf16[1024,1024]{1,0:T(8,128)(2,1)}, u32[]{:S(2)}) copy-start(bf16[1024,1024]{1,0:T(8,128)(2,1)} %all-gather.2.cloned.1.call-done) | copy-start | bytes 6291460
  129.3 124.0 %all-reduce.3.cloned.1.call-start = ((), (), s32[]{:S(2)}) async-start(), calls=%async_computation.3 | async-start | bytes 524288 | tf_op jit(solution)/shard_map/psum | solution.py:195
  134.4 17.6 %copy-start.17 = (bf16[128,1024]{1,0:T(8,128)(2,1)S(1)}, bf16[128,1024]{1,0:T(8,128)(2,1)}, u32[]{:S(2)}) copy-start(bf16[128,1024]{1,0:T(8,128)(2,1)} %get-tuple-element.102) | copy-start | bytes 786436
  139.6 13.3 %copy-start.18 = (bf16[128,1024]{1,0:T(8,128)(2,1)S(1)}, bf16[128,1024]{1,0:T(8,128)(2,1)}, u32[]{:S(2)}) copy-start(bf16[128,1024]{1,0:T(8,128)(2,1)} %get-tuple-element.104) | copy-start | bytes 786436
  142.7 48.9 %copy-start.16 = (bf16[128,1024]{1,0:T(8,128)(2,1)S(1)}, bf16[128,1024]{1,0:T(8,128)(2,1)}, u32[]{:S(2)}) copy-start(bf16[128,1024]{1,0:T(8,128)(2,1)} %param.16) | copy-start | bytes 786436
  192.8 9.6 %copy-start.37 = (f32[128,128]{1,0:T(8,128)S(1)}, f32[128,128]{1,0:T(8,128)}, u32[]{:S(2)}) copy-start(f32[128,128]{1,0:T(8,128)} %copy.73) | copy-start | bytes 196612
  192.8 10.2 %copy-start.36 = (f32[128,128]{0,1:T(8,128)S(1)}, f32[128,128]{0,1:T(8,128)}, u32[]{:S(2)}) copy-start(f32[128,128]{0,1:T(8,128)} %get-tuple-element.88) | copy-start | bytes 196612
  199.7 7.2 %copy-start.12 = (bf16[128,2048]{1,0:T(8,128)(2,1)S(1)}, bf16[128,2048]{1,0:T(8,128)(2,1)}, u32[]{:S(2)}) copy-start(bf16[128,2048]{1,0:T(8,128)(2,1)} %reduce-scatter.2.cloned.1.call-done) | copy-start | bytes 1572868
  203.2 51.9 %collective-permute-start.5 = (bf16[127,1024]{1,0:T(8,128)(2,1)S(1)}, bf16[127,1024]{1,0:T(8,128)(2,1)S(1)}, u32[]{:S(2)}, u32[]{:S(2)}) collective-permute-start(bf16[127,1024]{1,0:T(8,128)(2,1)S(1)} %slice.348), channel_id=1, source_target_pairs={{4,0},{8,4},{12,8},{16,12},{20,16},{24,20},{28,24},{5,1},{9,5},{13... | collective-permute-start | bytes 780296 | tf_op jit(solution)/shard_map/ppermute | solution.py:25
  255.3 7.0 %copy-start.4 = (bf16[128,1024]{1,0:T(8,128)(2,1)S(1)}, bf16[128,1024]{1,0:T(8,128)(2,1)}, u32[]{:S(2)}) copy-start(bf16[128,1024]{1,0:T(8,128)(2,1)} %copy-done.3) | copy-start | bytes 786436
  255.3 7.0 %copy-start.10 = (f32[1,128,1024]{2,0,1:T(1,128)S(1)}, f32[1,128,1024]{2,0,1:T(1,128)}, u32[]{:S(2)}) copy-start(f32[1,128,1024]{2,0,1:T(1,128)} %copy-done.9) | copy-start | bytes 1572868
  255.3 7.0 %copy-start.13 = (bf16[128,2048]{1,0:T(8,128)(2,1)S(1)}, bf16[128,2048]{1,0:T(8,128)(2,1)}, u32[]{:S(2)}) copy-start(bf16[128,2048]{1,0:T(8,128)(2,1)} %reduce-scatter.2.cloned.1.call-done) | copy-start | bytes 1572868
  255.3 7.0 %copy-start.20 = (bf16[128,1024]{1,0:T(8,128)(2,1)S(1)}, bf16[128,1024]{1,0:T(8,128)(2,1)}, u32[]{:S(2)}) copy-start(bf16[128,1024]{1,0:T(8,128)(2,1)} %param.17) | copy-start | bytes 786436
  289.6 3.1 %collective-permute-start.6 = (bf16[6,1024]{1,0:T(8,128)(2,1)S(1)}, bf16[6,1024]{1,0:T(8,128)(2,1)S(1)}, u32[]{:S(2)}, u32[]{:S(2)}) collective-permute-start(bf16[6,1024]{1,0:T(8,128)(2,1)S(1)} %slice.350), channel_id=1, source_target_pairs={{4,0},{8,4},{12,8},{16,12},{20,16},{24,20},{28,24},{5,1},{9,5},{13... | collective-permute-start | bytes 36872 | tf_op jit(solution)/shard_map/ppermute | solution.py:25
  (20 other events, 45.2 us)
Sparse Core Ops, SparseCore 0:
  21.5 29.0 all-gather.1
  129.4 49.2 reduce-scatter.1
  202.5 50.7 all-reduce.2
